TPU v7x, 32 devices: a whole 2x2x4 slice. The times are simulated.
32 devices in a mesh: parts: 2 (over x), ref: 16 (over z, y, core).
Axes of the slice: x: 2, y: 2, z: 4, core: 2. Of those that a mesh axis runs over, the one named last changes fastest.
Arguments:
- queries: float32 [4096, 128], P('parts'), parts along dimension 0, may hold values from -15 to 15, as said below
- references: float32 [65536, 128], P(('parts', 'ref')), parts along dimension 0, may hold values from -15 to 15
- query_ids: int32 [4096], P('parts'), parts along dimension 0, may hold values from 0 to 32767, as said below
- spread: float32 [128], replicated, may hold values from 0.5 to 2
- cotangent: float32 [4096], P('parts'), parts along dimension 0, may hold values from -4 to 4
Outputs:
- query_grad: float32 [4096, 128], P(('parts', 'ref')), parts along dimension 0
- reference_grad: float32 [65536, 128], P(('parts', 'ref')), parts along dimension 0
- spread_grad: float32 [256], P('parts'), parts along dimension 0
There are 2 independent parts, one for each index of `parts`. A program takes and returns all parts, laid end to end along the dimension named above; an argument that names none is the same for every part. Nothing has to cross between parts.
Inputs may be any that keep to these rules, and one draw needn't show every extreme that they name: `query_ids`: distinct rows of the references; query i is the reference row query_ids_i. `queries`: row i equals row query_ids_i of references.
All inputs are finite; a program needn't handle non-finite values.
Results may differ from a plain program's by a relative error of at most 0.014.
Values sent between devices are 32-bit elements; how exact they have to be, the bound alone decides.
No kernel may reach another device: no remote copies, remote signals or barrier semaphores. Data moves between devices by JAX's collectives and lax.ppermute only.
A program may use at most 64 MiB of HBM per device.

v0:
```python
import jax
import jax.numpy as jnp
from jax import lax
from jax.sharding import PartitionSpec as P


def block_score(query_block, id_block, references, rnorm, inv, ref_start):
    cross = lax.dot_general(
        query_block * inv,
        references,
        (((1,), (1,)), ((), ())),
        precision=lax.Precision.HIGHEST,
        preferred_element_type=jnp.float32,
    )
    qnorm = jnp.sum(query_block * query_block * inv, axis=1)
    score = cross - 0.5 * qnorm[:, None] - 0.5 * rnorm[None, :]
    local_ids = id_block - ref_start
    self_mask = local_ids[:, None] == lax.iota(jnp.int32, references.shape[0])[None, :]
    return (jnp.where(self_mask, -jnp.inf, score), self_mask)


def on_device(queries, references, query_ids, spread, cotangent):
    n_query = queries.shape[0]
    n_feat = queries.shape[1]
    n_ref = references.shape[0]
    block_rows = min(512, n_query)
    n_blocks = n_query // block_rows
    inv = 1.0 / (spread * spread)
    rnorm = jnp.sum(references * references * inv, axis=1)
    ref_start = lax.axis_index("ref") * n_ref
    query_blocks = queries.reshape(n_blocks, block_rows, n_feat)
    id_blocks = query_ids.reshape(n_blocks, block_rows)
    weight_blocks = cotangent.reshape(n_blocks, block_rows)

    def local_density(items):
        query_block, id_block = items
        score, self_mask = block_score(query_block, id_block, references, rnorm, inv, ref_start)
        local_peak = jnp.max(score, axis=1)
        local_total = jnp.sum(jnp.exp(score - local_peak[:, None]), axis=1)
        return (local_peak, local_total)

    local_peak, local_total = lax.map(local_density, (query_blocks, id_blocks))
    local_peak = local_peak.reshape(n_query)
    local_total = local_total.reshape(n_query)
    peak = lax.pmax(local_peak, "ref")
    total = lax.psum(local_total * jnp.exp(local_peak - peak), "ref")
    ref_low = references.astype(jnp.bfloat16)
    query_low_blocks = query_blocks.astype(jnp.bfloat16)

    def backward(carry, items):
        pushed, column = carry
        query_block, query_low, id_block, cot_block, peak_block, total_block = items
        score, self_mask = block_score(query_block, id_block, references, rnorm, inv, ref_start)
        weight = jnp.where(
            self_mask,
            0.0,
            cot_block[:, None] * jnp.exp(score - peak_block[:, None]) / total_block[:, None],
        ).astype(jnp.bfloat16)
        pulled = jnp.dot(weight, ref_low, preferred_element_type=jnp.float32)
        pushed = pushed + lax.dot_general(
            weight, query_low, (((0,), (0,)), ((), ())), preferred_element_type=jnp.float32
        )
        column = column + jnp.sum(weight.astype(jnp.float32), axis=0)
        return ((pushed, column), pulled)

    init = (jnp.zeros((n_ref, n_feat), jnp.float32), jnp.zeros((n_ref,), jnp.float32))
    items = (
        query_blocks,
        query_low_blocks,
        id_blocks,
        weight_blocks,
        peak.reshape(n_blocks, block_rows),
        total.reshape(n_blocks, block_rows),
    )
    (pushed, column), pulled = lax.scan(backward, init, items)
    pulled = pulled.reshape(n_query, n_feat)
    reference_grad = (pushed - references * column[:, None]) * inv
    ref_terms = jnp.sum(references * reference_grad, axis=0)
    weight_total = jnp.sum(cotangent)
    own_rows = n_query // lax.axis_size("ref")
    own_start = lax.axis_index("ref") * own_rows
    summed_pull, summed_terms = lax.psum((pulled, ref_terms), "ref")
    every_grad = (summed_pull - queries * cotangent[:, None]) * inv
    summed = jnp.sum(queries * every_grad, axis=0) + summed_terms
    query_grad = lax.dynamic_slice_in_dim(every_grad, own_start, own_rows, 0)
    spread_grad = -summed / spread - weight_total / spread
    return (query_grad, reference_grad, spread_grad)


def solution(mesh):
    placed = (P("parts", None), P(("parts", "ref"), None), P("parts"), P(), P("parts"))
    return jax.shard_map(
        on_device,
        mesh=mesh,
        in_specs=placed,
        out_specs=(P(("parts", "ref"), None), P(("parts", "ref"), None), P("parts")),
        check_vma=False,
    )
```

profile of v0, /device:TPU:0, one launch (start us, length us, event | category | flops | bytes accessed | tf_op | source)
XLA Modules:
  0.0 282.6 jit_solution(32626793319487471)
XLA Ops:
  7.2 0.0 all-reduce.2.cloned.1.call-start
  7.3 0.7 multiply_divide_fusion
  7.9 0.7 reshape.72
  8.6 0.7 reshape.73
  9.3 1.3 convert_element_type.12
  10.6 1.9 fusion.15
  12.5 30.2 %while.27 = (s32[]{:T(128)}, f32[4,512]{1,0:T(4,128)S(1)}, f32[4,512]{1,0:T(4,128)S(1)}, s32[4,512]{1,0:T(4,128)S(1)}, s32[]{:T(128)}, /*index=5*/f32[4,512,128]...) while((s32[]{:T(128)}, f32[4,512]{1,0:T(4,128)S(1)}, ...), condition=%wide.region_5.6_spmd, body=%wide.region_1.5_spmd.sunk | while | flops 1618216448 | bytes 10015885 | solution.py:42
  12.6 1.1 fusion.32
  13.7 5.6 %fusion.33 = (f32[512]{0:T(512)S(1)}, f32[512,2048]{1,0:T(8,128)S(1)}) fusion(f32[2048]{0:T(1024)S(1)} %broadcast_multiply_fusion.8, f32[512]{0:T(512)S(1)} %broadcast_multiply_fusion.9, f32[2048,128]{1,0:T(8,128)} %get-tuple-element.432, f32[4,512,128]{2,1,0:T(8,128)} %get-tuple-element.430, s32[]{:T(128)S(6)} %copy.16, ...), kind=kOutput, calls=%fused_computation.45.clone.1 | convolution fusion | flops 1615920640 | bytes 5519876 | tf_op jit(solution)/shard_map/while/body/eval_jaxpr/dot_general | solution.py:8
  19.3 0.7 exponential_reduce_fusion.2
  20.0 0.1 dynamic_update_slice.17
  20.1 1.1 fusion.32
  21.2 5.6 %fusion.33 = (f32[512]{0:T(512)S(1)}, f32[512,2048]{1,0:T(8,128)S(1)}) fusion(f32[2048]{0:T(1024)S(1)} %broadcast_multiply_fusion.8, f32[512]{0:T(512)S(1)} %broadcast_multiply_fusion.9, f32[2048,128]{1,0:T(8,128)} %get-tuple-element.432, f32[4,512,128]{2,1,0:T(8,128)} %get-tuple-element.430, s32[]{:T(128)S(6)} %copy.16, ...), kind=kOutput, calls=%fused_computation.45.clone.1 | convolution fusion | flops 1615920640 | bytes 5519876 | tf_op jit(solution)/shard_map/while/body/eval_jaxpr/dot_general | solution.py:8
  26.8 0.7 exponential_reduce_fusion.2
  27.6 0.1 dynamic_update_slice.17
  27.7 1.1 fusion.32
  28.8 5.6 %fusion.33 = (f32[512]{0:T(512)S(1)}, f32[512,2048]{1,0:T(8,128)S(1)}) fusion(f32[2048]{0:T(1024)S(1)} %broadcast_multiply_fusion.8, f32[512]{0:T(512)S(1)} %broadcast_multiply_fusion.9, f32[2048,128]{1,0:T(8,128)} %get-tuple-element.432, f32[4,512,128]{2,1,0:T(8,128)} %get-tuple-element.430, s32[]{:T(128)S(6)} %copy.16, ...), kind=kOutput, calls=%fused_computation.45.clone.1 | convolution fusion | flops 1615920640 | bytes 5519876 | tf_op jit(solution)/shard_map/while/body/eval_jaxpr/dot_general | solution.py:8
  34.4 0.7 exponential_reduce_fusion.2
  35.1 0.1 dynamic_update_slice.17
  35.2 1.1 fusion.32
  36.3 5.6 %fusion.33 = (f32[512]{0:T(512)S(1)}, f32[512,2048]{1,0:T(8,128)S(1)}) fusion(f32[2048]{0:T(1024)S(1)} %broadcast_multiply_fusion.8, f32[512]{0:T(512)S(1)} %broadcast_multiply_fusion.9, f32[2048,128]{1,0:T(8,128)} %get-tuple-element.432, f32[4,512,128]{2,1,0:T(8,128)} %get-tuple-element.430, s32[]{:T(128)S(6)} %copy.16, ...), kind=kOutput, calls=%fused_computation.45.clone.1 | convolution fusion | flops 1615920640 | bytes 5519876 | tf_op jit(solution)/shard_map/while/body/eval_jaxpr/dot_general | solution.py:8
  41.9 0.7 exponential_reduce_fusion.2
  42.7 0.1 dynamic_update_slice.17
  42.8 35.5 %pmax.7 = f32[2048]{0:T(1024)S(1)} all-reduce(f32[2048]{0:T(1024)S(1)} %bitcast.87), channel_id=1, replica_groups=mesh['parts'=2,'ref'=16] {'ref'}, use_global_device_ids=true, to_apply=%region_6.7 | all-reduce | flops 2048 | bytes 16384 | tf_op jit(solution)/shard_map/pmax | solution.py:45
  78.3 30.2 %psum.21 = f32[4,512]{1,0:T(4,128)S(1)} all-reduce(f32[4,512]{1,0:T(4,128)S(1)} %reshape.78), channel_id=1, replica_groups=mesh['parts'=2,'ref'=16] {'ref'}, use_global_device_ids=true, to_apply=%region_7.8 | all-reduce | flops 2048 | bytes 16384 | tf_op jit(solution)/shard_map/psum | solution.py:46
  108.5 40.9 %while.28 = (s32[]{:T(128)}, f32[2048,128]{1,0:T(8,128)S(1)}, f32[2048]{0:T(1024)S(1)}, f32[4,512,128]{2,1,0:T(8,128)}, s32[4,512]{1,0:T(4,128)S(1)}, /*index=5*...) while((s32[]{:T(128)}, f32[2048,128]{1,0:T(8,128)S(1)}, ...), condition=%wide.region_11.12_spmd.clone, body=%wide.region_8.11_spmd.clone.sunk | while | flops 2159809024 | bytes 10970320 | solution.py:75
  108.5 1.1 fusion.39
  109.7 6.4 %convert_reduce_fusion.2 = (f32[2048]{0:T(1024)S(1)}, bf16[512,2048]{1,0:T(8,128)(2,1)S(1)}) fusion(f32[512]{0:T(512)S(1)} %bitcast.89, f32[512]{0:T(512)S(1)} %bitcast.90, f32[2048]{0:T(1024)S(1)} %broadcast_multiply_fusion.10, f32[512]{0:T(512)S(1)} %broadcast_multiply_fusion.11, f32[2048,128]{1,0:T(8,128)} %get-tuple-element.479, ...), kind=kOutput, calls=%fused_computation.13.clone.1 | convolution fusion | flops 1622210560 | bytes 3435012 | tf_op jit(solution)/shard_map/while/body/eval_jaxpr/dot_general | solution.py:8
  116.1 1.2 convolution_add_fusion.2
  117.3 1.4 fusion.40
  118.7 1.1 fusion.39
  119.9 6.4 %convert_reduce_fusion.2 = (f32[2048]{0:T(1024)S(1)}, bf16[512,2048]{1,0:T(8,128)(2,1)S(1)}) fusion(f32[512]{0:T(512)S(1)} %bitcast.89, f32[512]{0:T(512)S(1)} %bitcast.90, f32[2048]{0:T(1024)S(1)} %broadcast_multiply_fusion.10, f32[512]{0:T(512)S(1)} %broadcast_multiply_fusion.11, f32[2048,128]{1,0:T(8,128)} %get-tuple-element.479, ...), kind=kOutput, calls=%fused_computation.13.clone.1 | convolution fusion | flops 1622210560 | bytes 3435012 | tf_op jit(solution)/shard_map/while/body/eval_jaxpr/dot_general | solution.py:8
  126.3 1.2 convolution_add_fusion.2
  127.5 1.4 fusion.40
  128.9 1.1 fusion.39
  130.1 6.4 %convert_reduce_fusion.2 = (f32[2048]{0:T(1024)S(1)}, bf16[512,2048]{1,0:T(8,128)(2,1)S(1)}) fusion(f32[512]{0:T(512)S(1)} %bitcast.89, f32[512]{0:T(512)S(1)} %bitcast.90, f32[2048]{0:T(1024)S(1)} %broadcast_multiply_fusion.10, f32[512]{0:T(512)S(1)} %broadcast_multiply_fusion.11, f32[2048,128]{1,0:T(8,128)} %get-tuple-element.479, ...), kind=kOutput, calls=%fused_computation.13.clone.1 | convolution fusion | flops 1622210560 | bytes 3435012 | tf_op jit(solution)/shard_map/while/body/eval_jaxpr/dot_general | solution.py:8
  136.5 1.2 convolution_add_fusion.2
  137.7 1.4 fusion.40
  139.1 1.1 fusion.39
  140.3 6.4 %convert_reduce_fusion.2 = (f32[2048]{0:T(1024)S(1)}, bf16[512,2048]{1,0:T(8,128)(2,1)S(1)}) fusion(f32[512]{0:T(512)S(1)} %bitcast.89, f32[512]{0:T(512)S(1)} %bitcast.90, f32[2048]{0:T(1024)S(1)} %broadcast_multiply_fusion.10, f32[512]{0:T(512)S(1)} %broadcast_multiply_fusion.11, f32[2048,128]{1,0:T(8,128)} %get-tuple-element.479, ...), kind=kOutput, calls=%fused_computation.13.clone.1 | convolution fusion | flops 1622210560 | bytes 3435012 | tf_op jit(solution)/shard_map/while/body/eval_jaxpr/dot_general | solution.py:8
  146.7 1.2 convolution_add_fusion.2
  147.9 1.4 fusion.40
  149.4 0.7 reduce_sum.75
  150.0 90.4 %all-reduce.2.cloned.1.call-done = f32[2048,128]{1,0:T(8,128)} async-done(((f32[2048,128]{1,0:T(8,128)}), f32[2048,128]{1,0:T(8,128)}) %all-reduce.2.cloned.1.call-update) | async-done | bytes 1048592 | tf_op jit(solution)/shard_map/psum | solution.py:82
  240.5 3.0 %multiply_reduce_fusion = (f32[128]{0:T(128)S(1)}, f32[2048,128]{1,0:T(8,128)}, f32[128]{0:T(128)S(1)}, f32[2048,128]{1,0:T(8,128)S(1)}) fusion(f32[2048,128]{1,0:T(8,128)} %get-tuple-element.491, f32[128]{0:T(128)S(1)} %get-tuple-element.498, f32[2048,128]{1,0:T(8,128)S(1)} %get-tuple-element.133, f32[2048]{0:T(1024)S(1)} %get-tuple-element.134, ...), kind=kLoop, calls=%fused_computation.36 | loop fusion | flops 2621184 | bytes 6309376 | tf_op jit(solution)/shard_map/reduce_sum | solution.py:78
  243.5 30.4 %psum.23 = f32[128]{0:T(128)S(1)} all-reduce(f32[128]{0:T(128)S(1)} %get-tuple-element.231), channel_id=1, replica_groups=mesh['parts'=2,'ref'=16] {'ref'}, use_global_device_ids=true, to_apply=%region_15.16 | all-reduce | flops 128 | bytes 1024 | tf_op jit(solution)/shard_map/psum | solution.py:82
  273.9 0.6 constant_dynamic-slice_fusion.3
  274.5 1.2 divide_subtract_fusion
  (55 shorter events, 0.5 us)
Async XLA Ops:
  7.2 233.3 %all-reduce.2.cloned.1.call-start = ((), (), s32[]{:S(2)}) async-start(), calls=%async_computation | async-start | bytes 2097152 | tf_op jit(solution)/shard_map/psum | solution.py:82
  108.5 40.9 %copy-start = (f32[2048]{0:T(1024)S(1)}, f32[2048]{0:T(1024)}, u32[]{:S(2)}) copy-start(f32[2048]{0:T(1024)} %param.13) | copy-start | bytes 24580
  149.3 125.2 %copy-start.1 = (f32[128]{0:T(128)S(1)}, f32[128]{0:T(128)}, u32[]{:S(2)}) copy-start(f32[128]{0:T(128)} %param.12) | copy-start | bytes 1540
Sparse Core Ops, SparseCore 0:
  149.5 90.9 all-reduce.1
where the time goes:
time: 283 us
  blocking collectives  96.1 us (34%)
  waiting for transfers between devices  90.5 us (32%)
  matrix products  58.4 us (21%)
  other arithmetic  20.5 us (7%)
  between operations  14.2 us (5%)
    psum x1, waiting for transfers between devices, on_device(): summed_pull, summed_terms = lax.psum((pulled, ref_terms), 'ref')  90.4 us
    dot_general x8, matrix products, block_score(): lax.dot_general(query_block * inv, references, (((1,), (1,)), ((), ())),...  47.9 us
    pmax x1, blocking collectives, on_device(): peak = lax.pmax(local_peak, 'ref')  35.5 us
    psum x1, blocking collectives, on_device(): summed_pull, summed_terms = lax.psum((pulled, ref_terms), 'ref')  30.4 us
    psum x1, blocking collectives, on_device(): total = lax.psum(local_total * jnp.exp(local_peak - peak), 'ref')  30.2 us
    reduce_sum x8, other arithmetic, block_score(): qnorm = jnp.sum(query_block * query_block * inv, axis=1)  8.81 us
    dot_general x4, matrix products, backward(): pulled = jnp.dot(weight, ref_low, preferred_element_type=jnp.float32)  5.7 us
  transfers between devices with their start and end apart: 1, of which 1 were waited for; matrix products, arithmetic and copies ran while one was open for 0% of the time, Pallas kernels for 0%

commit v1 on v0

--- a/solution.py
+++ b/solution.py
@@ -43,7 +43,9 @@
     local_peak = local_peak.reshape(n_query)
     local_total = local_total.reshape(n_query)
     peak = lax.pmax(local_peak, "ref")
-    total = lax.psum(local_total * jnp.exp(local_peak - peak), "ref")
+    unit = local_total * jnp.exp(local_peak - peak)
+    work_now = lax.all_gather(unit, axis_name="ref")
+    total = jnp.sum(work_now, 0)
     ref_low = references.astype(jnp.bfloat16)
     query_low_blocks = query_blocks.astype(jnp.bfloat16)
 

time: 283 us -> 272 us (0.961)
  blocking collectives: 96.1 us -> 83.5 us
    psum x1 -> x0, blocking collectives: 30.2 us -> none  [on_device(): total = lax.psum(local_total * jnp.exp(local_peak - peak), 'ref')]
    all_gather x0 -> x1, blocking collectives: none -> 17.7 us  [on_device(): work_now = lax.all_gather(unit, axis_name='ref')]
where the time goes in v1:
time: 272 us
  waiting for transfers between devices  91.9 us (34%)
  blocking collectives  83.5 us (31%)
  matrix products  58.4 us (21%)
  other arithmetic  20.6 us (8%)
  between operations  14.2 us (5%)
    psum x1, waiting for transfers between devices, on_device(): summed_pull, summed_terms = lax.psum((pulled, ref_terms), 'ref')  91.9 us
    dot_general x8, matrix products, block_score(): lax.dot_general(query_block * inv, references, (((1,), (1,)), ((), ())),...  47.9 us
    pmax x1, blocking collectives, on_device(): peak = lax.pmax(local_peak, 'ref')  35.5 us
    psum x1, blocking collectives, on_device(): summed_pull, summed_terms = lax.psum((pulled, ref_terms), 'ref')  30.4 us
    all_gather x1, blocking collectives, on_device(): work_now = lax.all_gather(unit, axis_name='ref')  17.7 us
    reduce_sum x8, other arithmetic, block_score(): qnorm = jnp.sum(query_block * query_block * inv, axis=1)  8.81 us
    dot_general x4, matrix products, backward(): pulled = jnp.dot(weight, ref_low, preferred_element_type=jnp.float32)  5.7 us
  transfers between devices with their start and end apart: 1, of which 1 were waited for; matrix products, arithmetic and copies ran while one was open for 0% of the time, Pallas kernels for 0%

profile of v1, /device:TPU:0, one launch (start us, length us, event | category | flops | bytes accessed | tf_op | source)
XLA Modules:
  0.0 271.6 jit_solution(3731734360498518854)
XLA Ops:
  7.2 0.0 all-reduce.2.cloned.1.call-start
  7.3 0.7 multiply_divide_fusion
  7.9 0.7 reshape.72
  8.6 0.7 reshape.73
  9.3 1.3 convert_element_type.12
  10.6 1.9 fusion.15
  12.5 30.2 %while.27 = (s32[]{:T(128)}, f32[4,512]{1,0:T(4,128)S(1)}, f32[4,512]{1,0:T(4,128)S(1)}, s32[4,512]{1,0:T(4,128)S(1)}, s32[]{:T(128)}, /*index=5*/f32[4,512,128]...) while((s32[]{:T(128)}, f32[4,512]{1,0:T(4,128)S(1)}, ...), condition=%wide.region_5.6_spmd, body=%wide.region_1.5_spmd.sunk | while | flops 1618216448 | bytes 10015885 | solution.py:42
  12.6 1.1 fusion.32
  13.7 5.6 %fusion.33 = (f32[512]{0:T(512)S(1)}, f32[512,2048]{1,0:T(8,128)S(1)}) fusion(f32[2048]{0:T(1024)S(1)} %broadcast_multiply_fusion.8, f32[512]{0:T(512)S(1)} %broadcast_multiply_fusion.9, f32[2048,128]{1,0:T(8,128)} %get-tuple-element.432, f32[4,512,128]{2,1,0:T(8,128)} %get-tuple-element.430, s32[]{:T(128)S(6)} %copy.16, ...), kind=kOutput, calls=%fused_computation.45.clone.1 | convolution fusion | flops 1615920640 | bytes 5519876 | tf_op jit(solution)/shard_map/while/body/eval_jaxpr/dot_general | solution.py:8
  19.3 0.7 exponential_reduce_fusion.2
  20.0 0.1 dynamic_update_slice.17
  20.1 1.1 fusion.32
  21.2 5.6 %fusion.33 = (f32[512]{0:T(512)S(1)}, f32[512,2048]{1,0:T(8,128)S(1)}) fusion(f32[2048]{0:T(1024)S(1)} %broadcast_multiply_fusion.8, f32[512]{0:T(512)S(1)} %broadcast_multiply_fusion.9, f32[2048,128]{1,0:T(8,128)} %get-tuple-element.432, f32[4,512,128]{2,1,0:T(8,128)} %get-tuple-element.430, s32[]{:T(128)S(6)} %copy.16, ...), kind=kOutput, calls=%fused_computation.45.clone.1 | convolution fusion | flops 1615920640 | bytes 5519876 | tf_op jit(solution)/shard_map/while/body/eval_jaxpr/dot_general | solution.py:8
  26.8 0.7 exponential_reduce_fusion.2
  27.6 0.1 dynamic_update_slice.17
  27.7 1.1 fusion.32
  28.8 5.6 %fusion.33 = (f32[512]{0:T(512)S(1)}, f32[512,2048]{1,0:T(8,128)S(1)}) fusion(f32[2048]{0:T(1024)S(1)} %broadcast_multiply_fusion.8, f32[512]{0:T(512)S(1)} %broadcast_multiply_fusion.9, f32[2048,128]{1,0:T(8,128)} %get-tuple-element.432, f32[4,512,128]{2,1,0:T(8,128)} %get-tuple-element.430, s32[]{:T(128)S(6)} %copy.16, ...), kind=kOutput, calls=%fused_computation.45.clone.1 | convolution fusion | flops 1615920640 | bytes 5519876 | tf_op jit(solution)/shard_map/while/body/eval_jaxpr/dot_general | solution.py:8
  34.4 0.7 exponential_reduce_fusion.2
  35.1 0.1 dynamic_update_slice.17
  35.2 1.1 fusion.32
  36.3 5.6 %fusion.33 = (f32[512]{0:T(512)S(1)}, f32[512,2048]{1,0:T(8,128)S(1)}) fusion(f32[2048]{0:T(1024)S(1)} %broadcast_multiply_fusion.8, f32[512]{0:T(512)S(1)} %broadcast_multiply_fusion.9, f32[2048,128]{1,0:T(8,128)} %get-tuple-element.432, f32[4,512,128]{2,1,0:T(8,128)} %get-tuple-element.430, s32[]{:T(128)S(6)} %copy.16, ...), kind=kOutput, calls=%fused_computation.45.clone.1 | convolution fusion | flops 1615920640 | bytes 5519876 | tf_op jit(solution)/shard_map/while/body/eval_jaxpr/dot_general | solution.py:8
  41.9 0.7 exponential_reduce_fusion.2
  42.7 0.1 dynamic_update_slice.17
  42.8 35.5 %pmax.7 = f32[2048]{0:T(1024)S(1)} all-reduce(f32[2048]{0:T(1024)S(1)} %bitcast.87), channel_id=1, replica_groups=mesh['parts'=2,'ref'=16] {'ref'}, use_global_device_ids=true, to_apply=%region_6.7 | all-reduce | flops 2048 | bytes 16384 | tf_op jit(solution)/shard_map/pmax | solution.py:45
  78.3 17.7 %all-gather = f32[32768]{0:T(1024)S(1)} all-gather(f32[2048]{0:T(1024)S(1)} %exponential_multiply_fusion), channel_id=2, replica_groups=mesh['parts'=2,'ref'=16] {'ref'}, dimensions={0}, use_global_device_ids=true | all-gather | bytes 139264 | tf_op jit(solution)/shard_map/all_gather | solution.py:47
  96.0 40.8 %while.28 = (s32[]{:T(128)}, f32[2048,128]{1,0:T(8,128)S(1)}, f32[2048]{0:T(1024)S(1)}, f32[4,512,128]{2,1,0:T(8,128)}, s32[4,512]{1,0:T(4,128)S(1)}, /*index=5*...) while((s32[]{:T(128)}, f32[2048,128]{1,0:T(8,128)S(1)}, ...), condition=%wide.region_11.12_spmd.clone, body=%wide.region_8.11_spmd.clone.sunk | while | flops 2159809024 | bytes 10970320 | solution.py:77
  96.1 1.1 fusion.39
  97.2 6.4 %convert_reduce_fusion.2 = (f32[2048]{0:T(1024)S(1)}, bf16[512,2048]{1,0:T(8,128)(2,1)S(1)}) fusion(f32[512]{0:T(512)S(1)} %bitcast.89, f32[512]{0:T(512)S(1)} %bitcast.90, f32[2048]{0:T(1024)S(1)} %broadcast_multiply_fusion.10, f32[512]{0:T(512)S(1)} %broadcast_multiply_fusion.11, f32[2048,128]{1,0:T(8,128)} %get-tuple-element.479, ...), kind=kOutput, calls=%fused_computation.13.clone.1 | convolution fusion | flops 1622210560 | bytes 3435012 | tf_op jit(solution)/shard_map/while/body/eval_jaxpr/dot_general | solution.py:8
  103.6 1.2 convolution_add_fusion.2
  104.8 1.4 fusion.40
  106.3 1.1 fusion.39
  107.4 6.4 %convert_reduce_fusion.2 = (f32[2048]{0:T(1024)S(1)}, bf16[512,2048]{1,0:T(8,128)(2,1)S(1)}) fusion(f32[512]{0:T(512)S(1)} %bitcast.89, f32[512]{0:T(512)S(1)} %bitcast.90, f32[2048]{0:T(1024)S(1)} %broadcast_multiply_fusion.10, f32[512]{0:T(512)S(1)} %broadcast_multiply_fusion.11, f32[2048,128]{1,0:T(8,128)} %get-tuple-element.479, ...), kind=kOutput, calls=%fused_computation.13.clone.1 | convolution fusion | flops 1622210560 | bytes 3435012 | tf_op jit(solution)/shard_map/while/body/eval_jaxpr/dot_general | solution.py:8
  113.8 1.2 convolution_add_fusion.2
  115.0 1.4 fusion.40
  116.5 1.1 fusion.39
  117.6 6.4 %convert_reduce_fusion.2 = (f32[2048]{0:T(1024)S(1)}, bf16[512,2048]{1,0:T(8,128)(2,1)S(1)}) fusion(f32[512]{0:T(512)S(1)} %bitcast.89, f32[512]{0:T(512)S(1)} %bitcast.90, f32[2048]{0:T(1024)S(1)} %broadcast_multiply_fusion.10, f32[512]{0:T(512)S(1)} %broadcast_multiply_fusion.11, f32[2048,128]{1,0:T(8,128)} %get-tuple-element.479, ...), kind=kOutput, calls=%fused_computation.13.clone.1 | convolution fusion | flops 1622210560 | bytes 3435012 | tf_op jit(solution)/shard_map/while/body/eval_jaxpr/dot_general | solution.py:8
  124.0 1.2 convolution_add_fusion.2
  125.2 1.4 fusion.40
  126.7 1.1 fusion.39
  127.8 6.4 %convert_reduce_fusion.2 = (f32[2048]{0:T(1024)S(1)}, bf16[512,2048]{1,0:T(8,128)(2,1)S(1)}) fusion(f32[512]{0:T(512)S(1)} %bitcast.89, f32[512]{0:T(512)S(1)} %bitcast.90, f32[2048]{0:T(1024)S(1)} %broadcast_multiply_fusion.10, f32[512]{0:T(512)S(1)} %broadcast_multiply_fusion.11, f32[2048,128]{1,0:T(8,128)} %get-tuple-element.479, ...), kind=kOutput, calls=%fused_computation.13.clone.1 | convolution fusion | flops 1622210560 | bytes 3435012 | tf_op jit(solution)/shard_map/while/body/eval_jaxpr/dot_general | solution.py:8
  134.2 1.2 convolution_add_fusion.2
  135.4 1.4 fusion.40
  136.9 0.7 reduce_sum.85
  137.6 91.9 %all-reduce.2.cloned.1.call-done = f32[2048,128]{1,0:T(8,128)} async-done(((f32[2048,128]{1,0:T(8,128)}), f32[2048,128]{1,0:T(8,128)}) %all-reduce.2.cloned.1.call-update) | async-done | bytes 1048592 | tf_op jit(solution)/shard_map/psum | solution.py:84
  229.5 3.0 %multiply_reduce_fusion = (f32[128]{0:T(128)S(1)}, f32[2048,128]{1,0:T(8,128)}, f32[128]{0:T(128)S(1)}, f32[2048,128]{1,0:T(8,128)S(1)}) fusion(f32[2048,128]{1,0:T(8,128)} %get-tuple-element.491, f32[128]{0:T(128)S(1)} %get-tuple-element.498, f32[2048,128]{1,0:T(8,128)S(1)} %get-tuple-element.133, f32[2048]{0:T(1024)S(1)} %get-tuple-element.134, ...), kind=kLoop, calls=%fused_computation.36 | loop fusion | flops 2621184 | bytes 6309376 | tf_op jit(solution)/shard_map/reduce_sum | solution.py:80
  232.4 30.4 %psum.15 = f32[128]{0:T(128)S(1)} all-reduce(f32[128]{0:T(128)S(1)} %get-tuple-element.231), channel_id=1, replica_groups=mesh['parts'=2,'ref'=16] {'ref'}, use_global_device_ids=true, to_apply=%region_15.16 | all-reduce | flops 128 | bytes 1024 | tf_op jit(solution)/shard_map/psum | solution.py:84
  262.9 0.6 constant_dynamic-slice_fusion.3
  263.5 1.2 divide_subtract_fusion
  (57 shorter events, 0.5 us)
Async XLA Ops:
  7.2 222.3 %all-reduce.2.cloned.1.call-start = ((), (), s32[]{:S(2)}) async-start(), calls=%async_computation | async-start | bytes 2097152 | tf_op jit(solution)/shard_map/psum | solution.py:84
  96.0 40.9 %copy-start = (f32[2048]{0:T(1024)S(1)}, f32[2048]{0:T(1024)}, u32[]{:S(2)}) copy-start(f32[2048]{0:T(1024)} %param.13) | copy-start | bytes 24580
  136.8 126.6 %copy-start.1 = (f32[128]{0:T(128)S(1)}, f32[128]{0:T(128)}, u32[]{:S(2)}) copy-start(f32[128]{0:T(128)} %param.12) | copy-start | bytes 1540
Sparse Core Ops, SparseCore 0:
  137.0 92.4 all-reduce.1
